TPU v7x, 32 devices: a whole 2x2x4 slice. The times are simulated.
32 devices in a mesh: grp: 4 (over z), emb: 8 (over y, x, core).
Axes of the slice: x: 2, y: 2, z: 4, core: 2. Of those that a mesh axis runs over, the one named last changes fastest.
Arguments:
- bottom_out: bfloat16 [4096, 128], P(('grp', 'emb')), may hold values from -6 to 6
- owner_ids: int32 [106496, 1], P(('grp', 'emb')), may hold values from 0 to 7; in each aligned block of 3328 rows (0 to 3327, 3328 to 6655, ...) at most 624 rows name the same one
- row_ids: int32 [4096, 26], P(('grp', 'emb')), may hold values from 0 to 95
- positions: int32 [4096], P(('grp', 'emb')), may hold values from 0 to 15
- labels: int32 [4096], P(('grp', 'emb')), may hold values 0 or 1
- tables: bfloat16 [26, 768, 128], P(None, 'emb'), may hold values from -6 to 6
- cross_down: bfloat16 [3456, 512], replicated, may hold values from -0.109375 to 0.109375
- cross_up: bfloat16 [512, 3456], replicated, may hold values from -0.25 to 0.25
- cross_bias: float32 [3456], replicated, may hold values from -3 to 3
- out_weight: bfloat16 [3456], replicated, may hold values from -0.109375 to 0.109375
- position_bias: float32 [16], replicated, may hold values from -2 to 2
Outputs:
- table_grad: float32 [26, 768, 128], P(None, 'emb')
- bottom_grad: bfloat16 [4096, 128], P(('grp', 'emb'))
- bias_grad: float32 [3456], replicated
Inputs may be any that keep to these rules, and one draw needn't show every extreme that they name: `owner_ids`: in every aligned block of 3328 lookups (the lookups of one device) no owner is named more than 624 times, and in some block one owner is named exactly 624 times.
All inputs are finite; a program needn't handle non-finite values. No bound on the sum of `labels` on one device may be relied on, other than what follows from the above.
Results may differ from a plain program's by a relative error of at most 0.0085.
Values may be sent and summed in bfloat16 or wider, within the bound.
No kernel may reach another device: no remote copies, remote signals or barrier semaphores. Data moves between devices by JAX's collectives and lax.ppermute only.
A program may use at most 64 MiB of HBM per device.

v0:
```python
import jax
import jax.numpy as jnp
from jax import lax
from jax.sharding import PartitionSpec as P


def local(
    bottom_out,
    owner_ids,
    row_ids,
    positions,
    labels,
    tables,
    cross_down,
    cross_up,
    cross_bias,
    out_weight,
    position_bias,
):
    sample_count, table_count = row_ids.shape
    rows_local = tables.shape[1]
    row_width = tables.shape[2]
    owner_count = lax.axis_size("emb")
    capacity = 3 * sample_count * table_count // (2 * owner_count)
    lookup_count = sample_count * table_count
    owners = owner_ids.reshape(sample_count, table_count)
    flat_owner = owners.reshape(-1)
    local_grid = jnp.arange(table_count, dtype=jnp.int32)[None, :] * rows_local + row_ids
    local_index = local_grid.reshape(-1)
    owner_marks = (flat_owner[:, None] == jnp.arange(owner_count, dtype=jnp.int32)[None, :]).astype(
        jnp.int32
    )
    ranking = jnp.cumsum(owner_marks, axis=0) - 1
    slot_index = jnp.sum(ranking * owner_marks, axis=1)
    buffer_place = flat_owner * capacity + slot_index
    flat_table = tables.reshape(table_count * rows_local, row_width)
    request = jnp.zeros((owner_count * capacity,), jnp.int32).at[buffer_place].set(local_index)
    request = request.reshape(owner_count, capacity)
    received = lax.all_to_all(request, "emb", split_axis=0, concat_axis=0, tiled=True)
    fetched = flat_table[received]
    arrived = lax.all_to_all(fetched, "emb", split_axis=0, concat_axis=0, tiled=True)
    pooled = arrived.reshape(owner_count * capacity, row_width)[buffer_place].reshape(
        sample_count, table_count * row_width
    )
    first = jnp.concatenate([bottom_out, pooled], axis=1)
    first_wide = first.astype(jnp.float32)
    weight_row = out_weight.astype(jnp.float32)
    reduced = jnp.dot(first, cross_down, preferred_element_type=jnp.float32).astype(jnp.bfloat16)
    gate_scale = jnp.dot(reduced, cross_up, preferred_element_type=jnp.float32) + cross_bias
    crossed = first_wide * gate_scale + first_wide
    position_marks = (
        positions[:, None] == jnp.arange(position_bias.shape[0], dtype=jnp.int32)[None, :]
    ).astype(jnp.float32)
    logit = jnp.sum(crossed * weight_row[None, :], axis=1) + jnp.sum(
        position_marks * position_bias[None, :], axis=1
    )
    err = jax.nn.sigmoid(logit) - labels.astype(jnp.float32)
    cotangent = err[:, None] * weight_row[None, :]
    scaled = cotangent * first_wide
    down_grad = lax.dot_general(
        scaled.astype(jnp.bfloat16),
        cross_up,
        (((1,), (1,)), ((), ())),
        preferred_element_type=jnp.float32,
    ).astype(jnp.bfloat16)
    back_term = lax.dot_general(
        down_grad, cross_down, (((1,), (1,)), ((), ())), preferred_element_type=jnp.float32
    )
    input_grad = (cotangent * (gate_scale + 1.0) + back_term).astype(jnp.bfloat16)
    bottom_grad = input_grad[:, :row_width]
    row_grads = input_grad[:, row_width:].reshape(lookup_count, row_width)
    outgoing = (
        jnp.zeros((owner_count * capacity, row_width), jnp.bfloat16).at[buffer_place].set(row_grads)
    )
    incoming = lax.all_to_all(
        outgoing.reshape(owner_count, capacity, row_width),
        "emb",
        split_axis=0,
        concat_axis=0,
        tiled=True,
    )
    local_grad = (
        jnp.zeros((table_count * rows_local, row_width), jnp.float32)
        .at[received.reshape(-1)]
        .add(incoming.reshape(owner_count * capacity, row_width).astype(jnp.float32))
    )
    summed_grad = lax.psum(local_grad.astype(jnp.bfloat16), "grp").astype(jnp.float32)
    table_grad = summed_grad.reshape(table_count, rows_local, row_width)
    bias_local = jnp.sum(scaled, axis=0)
    bias_grad = lax.psum(bias_local, ("grp", "emb"))
    return (table_grad, bottom_grad, bias_grad)


def solution(mesh):
    placed = (
        P(("grp", "emb"), None),
        P(("grp", "emb"), None),
        P(("grp", "emb"), None),
        P(("grp", "emb")),
        P(("grp", "emb")),
        P(None, "emb", None),
        P(),
        P(),
        P(),
        P(),
        P(),
    )
    return jax.shard_map(
        local,
        mesh=mesh,
        in_specs=placed,
        out_specs=(P(None, "emb", None), P(("grp", "emb"), None), P()),
        check_vma=False,
    )
```

profile of v0, /device:TPU:0, one launch (start us, length us, event | category | flops | bytes accessed | tf_op | source)
XLA Modules:
  0.0 242.6 jit_solution(920060485825970964)
XLA Ops:
  8.9 1.6 reshape.157
  11.9 5.2 %reduce-window.6 = s32[8,26,128]{2,1,0:T(8,128)} reduce-window(s32[8,26,128]{2,1,0:T(8,128)} %fusion.17, s32[]{:T(128)} %constant.10.clone.1), window={size=1x1x128 pad=0_0x0_0x127_0}, to_apply=%region_0.0 | reduce-window | flops 3381248 | bytes 212996 | tf_op jit(solution)/shard_map/reduce-window
  17.1 1.8 slice_reduce_fusion
  18.9 1.5 reduce-window.9
  22.2 13.5 %scatter_custom_fusion = s32[4992]{0:T(1024)} fusion(s32[3328]{0:T(1024)S(1)} %fusion.22, s32[3328]{0:T(1024)} %reshape.157, s32[]{:T(128)} %constant.10.clone.1), kind=kCustom, calls=%fused_computation.40 | custom fusion | bytes 20480 | tf_op jit(solution)/shard_map/scatter | solution.py:37
  37.1 9.9 %all_to_all.22 = s32[8,1,624]{2,1,0:T(1,128)S(1)} all-to-all(s32[8,1,624]{2,1,0:T(1,128)} %all_to_all.14), channel_id=1, replica_groups=mesh['grp'=4,'emb'=8] {'emb'}, dimensions={0} | all-to-all | bytes 39936 | tf_op jit(solution)/shard_map/all_to_all | solution.py:39
  51.1 12.3 %gather_fusion = bf16[4992,128]{1,0:T(8,128)(2,1)} fusion(bf16[2496,128]{1,0:T(8,128)(2,1)} %bitcast.32, s32[5120]{0:T(1024)} %pad_clamp_fusion), kind=kCustom, calls=%fused_computation | custom fusion | bytes 2575872 | tf_op jit(solution)/shard_map/gather | solution.py:40
  63.4 4.3 %all-to-all-start.1 = ((bf16[8,624,128]{2,1,0:T(8,128)(2,1)}), bf16[8,624,128]{2,1,0:T(8,128)(2,1)}, u32[]{:S(2)}, u32[]{:S(2)}) async-start(bf16[8,624,128]{2,1,0:T(8,128)(2,1)} %bitcast.34), calls=%async_computation.1 | async-start | bytes 2555904 | tf_op jit(solution)/shard_map/all_to_all | solution.py:41
  72.3 13.2 %all-to-all-done.1 = bf16[8,624,128]{2,1,0:T(8,128)(2,1)} async-done(((bf16[8,624,128]{2,1,0:T(8,128)(2,1)}), bf16[8,624,128]{2,1,0:T(8,128)(2,1)}, u32[]{:S(2)}, u32[]{:S(2)}) %all-to-all-start.1) | async-done | bytes 1277984 | tf_op jit(solution)/shard_map/all_to_all | solution.py:41
  85.5 9.2 %gather_fusion.1 = bf16[3328,128]{1,0:T(8,128)(2,1)} fusion(bf16[4992,128]{1,0:T(8,128)(2,1)} %bitcast.4, s32[4096]{0:T(1024)} %pad_clamp_fusion.1), kind=kCustom, calls=%fused_computation.1 | custom fusion | bytes 1717248 | tf_op jit(solution)/shard_map/gather | solution.py:42
  94.7 2.8 %reshape.131 = bf16[128,3328]{1,0:T(8,128)(2,1)} reshape(bf16[3328,128]{1,0:T(8,128)(2,1)} %gather_fusion.1) | data formatting | bytes 1703936 | tf_op jit(solution)/shard_map/reshape | solution.py:42
  97.5 2.1 constant_dynamic-update-slice_fusion
  99.6 5.6 %fusion.6 = (f32[128]{0:T(128)}, f32[128,3456]{1,0:T(8,128)}) fusion(bf16[128,3456]{1,0:T(8,128)(2,1)} %constant_dynamic-update-slice_fusion, f32[3456]{0:T(1024)S(1)} %convert_element_type.40, f32[3456]{0:T(1024)} %param.19, bf16[512,3456]{1,0:T(8,128)(2,1)} %param.18, bf16[3456,512]{1,0:T(8,128)(2,1)S(1)} %copy-done), kind=kOutput, calls=%fused_computation.16 | convolution fusion | flops 908689280 | bytes 9760256 | tf_op jit(solution)/shard_map/dot_general | solution.py:49
  106.4 6.1 %fusion = bf16[128,3456]{1,0:T(8,128)(2,1)} fusion(bf16[3456,512]{1,0:T(8,128)(2,1)S(1)} %copy-done, f32[128,3456]{1,0:T(8,128)} %get-tuple-element.4, bf16[512,3456]{1,0:T(8,128)(2,1)} %param.18, bf16[128,3456]{1,0:T(8,128)(2,1)} %constant_dynamic-update-slice_fusion, f32[128]{0:T(128)} %divide_subtract_fusion, f32[3456]{0:T(1024)S(1)} %convert_element_type.40), kind=kOutput, calls=%fused_computation.7 | convolution fusion | flops 910016512 | bytes 10631168 | tf_op jit(solution)/shard_map/dot_general | solution.py:66
  112.4 2.1 slice.21
  114.5 2.9 %reshape.165 = bf16[3328,128]{1,0:T(8,128)(2,1)} reshape(bf16[128,3328]{1,0:T(8,128)(2,1)} %slice.21) | data formatting | bytes 1703936 | tf_op jit(solution)/shard_map/reshape | solution.py:71
  117.4 14.9 %scatter_custom_fusion.1 = bf16[4992,128]{1,0:T(8,128)(2,1)} fusion(s32[3328]{0:T(1024)} %copy-done.2, bf16[3328,128]{1,0:T(8,128)(2,1)} %reshape.165, bf16[]{:T(256)} %constant.5.clone.1), kind=kCustom, calls=%fused_computation.21 | custom fusion | bytes 1278464 | tf_op jit(solution)/shard_map/scatter | solution.py:73
  132.3 4.3 %all-to-all-start.2 = ((bf16[8,624,128]{2,1,0:T(8,128)(2,1)}), bf16[8,624,128]{2,1,0:T(8,128)(2,1)}, u32[]{:S(2)}, u32[]{:S(2)}) async-start(bf16[8,624,128]{2,1,0:T(8,128)(2,1)} %bitcast.33), calls=%async_computation.2 | async-start | bytes 2555904 | tf_op jit(solution)/shard_map/all_to_all | solution.py:75
  141.0 13.4 %all-to-all-done.2 = bf16[8,624,128]{2,1,0:T(8,128)(2,1)} async-done(((bf16[8,624,128]{2,1,0:T(8,128)(2,1)}), bf16[8,624,128]{2,1,0:T(8,128)(2,1)}, u32[]{:S(2)}, u32[]{:S(2)}) %all-to-all-start.2) | async-done | bytes 1277984 | tf_op jit(solution)/shard_map/all_to_all | solution.py:75
  154.4 33.9 %scatter_custom_fusion.2 = f32[2496,128]{1,0:T(8,128)} fusion(s32[4992]{0:T(1024)} %fusion.21, bf16[4992,128]{1,0:T(8,128)(2,1)} %bitcast.8, f32[]{:T(128)} %constant.9.clone.1), kind=kCustom, calls=%fused_computation.9 | custom fusion | flops 1277952 | bytes 2556416 | tf_op jit(solution)/shard_map/scatter-add | solution.py:85
  188.4 2.2 convert_element_type.47
  192.0 2.1 fusion.3
  194.1 39.5 %psum.15 = f32[3456]{0:T(1024)} all-reduce(f32[3456]{0:T(1024)} %fusion.3), channel_id=1, replica_groups=mesh['grp'=4,'emb'=8] {'grp','emb'}, use_global_device_ids=true, to_apply=%region_10.11 | all-reduce | flops 3456 | bytes 27648 | tf_op jit(solution)/shard_map/psum | solution.py:90
  233.5 2.3 reshape.135
  (30 shorter events, 22.1 us)
Async XLA Ops:
  7.2 92.5 %copy-start = (bf16[3456,512]{1,0:T(8,128)(2,1)S(1)}, bf16[3456,512]{1,0:T(8,128)(2,1)}, u32[]{:S(2)}) copy-start(bf16[3456,512]{1,0:T(8,128)(2,1)} %param.17) | copy-start | bytes 10616836
  22.2 41.2 %copy-start.2 = (s32[3328]{0:T(1024)}, s32[3328]{0:T(1024)S(1)}, u32[]{:S(2)}) copy-start(s32[3328]{0:T(1024)S(1)} %fusion.22) | copy-start | bytes 39940
  47.1 0.6 copy-start.1
  63.4 22.1 %all-to-all-start.1 = ((bf16[8,624,128]{2,1,0:T(8,128)(2,1)}), bf16[8,624,128]{2,1,0:T(8,128)(2,1)}, u32[]{:S(2)}, u32[]{:S(2)}) async-start(bf16[8,624,128]{2,1,0:T(8,128)(2,1)} %bitcast.34), calls=%async_computation.1 | async-start | bytes 2555904 | tf_op jit(solution)/shard_map/all_to_all | solution.py:41
  132.3 22.1 %all-to-all-start.2 = ((bf16[8,624,128]{2,1,0:T(8,128)(2,1)}), bf16[8,624,128]{2,1,0:T(8,128)(2,1)}, u32[]{:S(2)}, u32[]{:S(2)}) async-start(bf16[8,624,128]{2,1,0:T(8,128)(2,1)} %bitcast.33), calls=%async_computation.2 | async-start | bytes 2555904 | tf_op jit(solution)/shard_map/all_to_all | solution.py:75
  136.5 97.0 %all-reduce.2.cloned.1.call-start = ((), (), s32[]{:S(2)}) async-start(), calls=%async_computation.3 | async-start | bytes 1277952 | tf_op jit(solution)/shard_map/psum | solution.py:87
Sparse Core Ops, SparseCore 0:
  190.7 39.9 all-reduce.1
where the time goes:
time: 245 us; the launch traced here: 243 us
  local copies, waits for them, and re-layouts  71.5 us (29%)
  other arithmetic  60.6 us (25%)
  blocking collectives  49.4 us (20%)
  waiting for transfers between devices  26.7 us (11%)
  between operations  14.1 us (6%)
  matrix products  11.6 us (5%)
  starting transfers between devices  8.73 us (4%)
    psum x1, blocking collectives, local(): bias_grad = lax.psum(bias_local, ('grp', 'emb'))  39.5 us
    scatter-add x1, other arithmetic, local(): local_grad = jnp.zeros((table_count * rows_local, row_width), jnp.float32...  33.9 us
    scatter x1, local copies, waits for them, and re-layouts, local(): jnp.zeros((owner_count * capacity, row_width), jnp.bfloat16)  14.9 us
    scatter x1, local copies, waits for them, and re-layouts, local(): jnp.zeros((owner_count * capacity,), jnp.int32).at[buffer_place]  13.5 us
    all_to_all x1, waiting for transfers between devices, local(): lax.all_to_all(outgoing.reshape(owner_count, capacity, row_width), 'emb',...  13.4 us
    all_to_all x1, waiting for transfers between devices, local(): lax.all_to_all(fetched, 'emb', split_axis=0, concat_axis=0, tiled=True)  13.2 us
    gather x1, local copies, waits for them, and re-layouts, local(): fetched = flat_table[received]  12.3 us
    all_to_all x1, blocking collectives, local(): lax.all_to_all(request, 'emb', split_axis=0, concat_axis=0, tiled=True)  9.94 us
  transfers between devices with their start and end apart: 3, of which 2 were waited for; matrix products, arithmetic and copies ran while one was open for 5% of the time, Pallas kernels for 0%

commit v1 on v0

--- a/solution.py
+++ b/solution.py
@@ -2,6 +2,12 @@
 import jax.numpy as jnp
 from jax import lax
 from jax.sharding import PartitionSpec as P
+
+
+def summed_here(x, axis):
+    parts = lax.all_gather(x, axis, axis=0, tiled=False)
+    total = parts.sum(axis=0)
+    return total
 
 
 def local(
@@ -87,7 +93,7 @@
     summed_grad = lax.psum(local_grad.astype(jnp.bfloat16), "grp").astype(jnp.float32)
     table_grad = summed_grad.reshape(table_count, rows_local, row_width)
     bias_local = jnp.sum(scaled, axis=0)
-    bias_grad = lax.psum(bias_local, ("grp", "emb"))
+    bias_grad = summed_here(bias_local, ("grp", "emb"))
     return (table_grad, bottom_grad, bias_grad)
 
 

time: 245 us -> 250 us (1.020)
  blocking collectives: 49.4 us -> 53.2 us
    all_gather x0 -> x1, blocking collectives: none -> 43.2 us  [summed_here(): parts = lax.all_gather(x, axis, axis=0, tiled=False)]
    psum x1 -> x0, blocking collectives: 39.5 us -> none  [local(): bias_grad = lax.psum(bias_local, ('grp', 'emb'))]
  transfers between devices with their start and end apart: 3 -> 3, of which waited for: 2 -> 2; matrix products, arithmetic and copies ran while one was open for 5% -> 6% of each run, Pallas kernels for 0% -> 0%
where the time goes in v1:
time: 250 us; the launch traced here: 248 us
  local copies, waits for them, and re-layouts  71.5 us (29%)
  other arithmetic  62 us (25%)
  blocking collectives  53.2 us (21%)
  waiting for transfers between devices  26.6 us (11%)
  between operations  14.1 us (6%)
  matrix products  11.6 us (5%)
  starting transfers between devices  8.73 us (3%)
    all_gather x1, blocking collectives, summed_here(): parts = lax.all_gather(x, axis, axis=0, tiled=False)  43.2 us
    scatter-add x1, other arithmetic, local(): local_grad = jnp.zeros((table_count * rows_local, row_width), jnp.float32...  33.9 us
    scatter x1, local copies, waits for them, and re-layouts, local(): jnp.zeros((owner_count * capacity, row_width), jnp.bfloat16)  14.9 us
    scatter x1, local copies, waits for them, and re-layouts, local(): jnp.zeros((owner_count * capacity,), jnp.int32).at[buffer_place]  13.5 us
    all_to_all x1, waiting for transfers between devices, local(): lax.all_to_all(outgoing.reshape(owner_count, capacity, row_width), 'emb',...  13.4 us
    all_to_all x1, waiting for transfers between devices, local(): lax.all_to_all(fetched, 'emb', split_axis=0, concat_axis=0, tiled=True)  13.2 us
    gather x1, local copies, waits for them, and re-layouts, local(): fetched = flat_table[received]  12.3 us
    all_to_all x1, blocking collectives, local(): lax.all_to_all(request, 'emb', split_axis=0, concat_axis=0, tiled=True)  9.94 us
  transfers between devices with their start and end apart: 3, of which 2 were waited for; matrix products, arithmetic and copies ran while one was open for 6% of the time, Pallas kernels for 0%

profile of v1, /device:TPU:0, one launch (start us, length us, event | category | flops | bytes accessed | tf_op | source)
XLA Modules:
  0.0 247.7 jit_solution(1146338255413169811)
XLA Ops:
  8.9 1.6 reshape.157
  11.9 5.2 %reduce-window.6 = s32[8,26,128]{2,1,0:T(8,128)} reduce-window(s32[8,26,128]{2,1,0:T(8,128)} %fusion.17, s32[]{:T(128)} %constant.10.clone.1), window={size=1x1x128 pad=0_0x0_0x127_0}, to_apply=%region_0.0 | reduce-window | flops 3381248 | bytes 212996 | tf_op jit(solution)/shard_map/reduce-window
  17.1 1.8 slice_reduce_fusion
  22.2 13.5 %scatter_custom_fusion = s32[4992]{0:T(1024)} fusion(s32[3328]{0:T(1024)S(1)} %fusion.22, s32[3328]{0:T(1024)} %reshape.157, s32[]{:T(128)} %constant.10.clone.1), kind=kCustom, calls=%fused_computation.40 | custom fusion | bytes 20480 | tf_op jit(solution)/shard_map/scatter | solution.py:43
  37.1 9.9 %all_to_all.22 = s32[8,1,624]{2,1,0:T(1,128)S(1)} all-to-all(s32[8,1,624]{2,1,0:T(1,128)} %all_to_all.14), channel_id=1, replica_groups=mesh['grp'=4,'emb'=8] {'emb'}, dimensions={0} | all-to-all | bytes 39936 | tf_op jit(solution)/shard_map/all_to_all | solution.py:45
  51.1 12.3 %gather_fusion = bf16[4992,128]{1,0:T(8,128)(2,1)} fusion(bf16[2496,128]{1,0:T(8,128)(2,1)} %bitcast.32, s32[5120]{0:T(1024)} %pad_clamp_fusion), kind=kCustom, calls=%fused_computation | custom fusion | bytes 2575872 | tf_op jit(solution)/shard_map/gather | solution.py:46
  63.4 4.3 %all-to-all-start.1 = ((bf16[8,624,128]{2,1,0:T(8,128)(2,1)}), bf16[8,624,128]{2,1,0:T(8,128)(2,1)}, u32[]{:S(2)}, u32[]{:S(2)}) async-start(bf16[8,624,128]{2,1,0:T(8,128)(2,1)} %bitcast.34), calls=%async_computation.1 | async-start | bytes 2555904 | tf_op jit(solution)/shard_map/all_to_all | solution.py:47
  72.3 13.2 %all-to-all-done.1 = bf16[8,624,128]{2,1,0:T(8,128)(2,1)} async-done(((bf16[8,624,128]{2,1,0:T(8,128)(2,1)}), bf16[8,624,128]{2,1,0:T(8,128)(2,1)}, u32[]{:S(2)}, u32[]{:S(2)}) %all-to-all-start.1) | async-done | bytes 1277984 | tf_op jit(solution)/shard_map/all_to_all | solution.py:47
  85.5 9.2 %gather_fusion.1 = bf16[3328,128]{1,0:T(8,128)(2,1)} fusion(bf16[4992,128]{1,0:T(8,128)(2,1)} %bitcast.4, s32[4096]{0:T(1024)} %pad_clamp_fusion.1), kind=kCustom, calls=%fused_computation.1 | custom fusion | bytes 1717248 | tf_op jit(solution)/shard_map/gather | solution.py:48
  94.7 2.8 %reshape.131 = bf16[128,3328]{1,0:T(8,128)(2,1)} reshape(bf16[3328,128]{1,0:T(8,128)(2,1)} %gather_fusion.1) | data formatting | bytes 1703936 | tf_op jit(solution)/shard_map/reshape | solution.py:48
  97.5 2.1 constant_dynamic-update-slice_fusion
  99.6 5.6 %fusion.6 = (f32[128]{0:T(128)}, f32[128,3456]{1,0:T(8,128)}) fusion(bf16[128,3456]{1,0:T(8,128)(2,1)} %constant_dynamic-update-slice_fusion, f32[3456]{0:T(1024)S(1)} %convert_element_type.40, f32[3456]{0:T(1024)} %param.19, bf16[512,3456]{1,0:T(8,128)(2,1)} %param.18, bf16[3456,512]{1,0:T(8,128)(2,1)S(1)} %copy-done), kind=kOutput, calls=%fused_computation.16 | convolution fusion | flops 908689280 | bytes 9760256 | tf_op jit(solution)/shard_map/dot_general | solution.py:55
  106.4 6.1 %fusion = bf16[128,3456]{1,0:T(8,128)(2,1)} fusion(bf16[3456,512]{1,0:T(8,128)(2,1)S(1)} %copy-done, f32[128,3456]{1,0:T(8,128)} %get-tuple-element.4, bf16[512,3456]{1,0:T(8,128)(2,1)} %param.18, bf16[128,3456]{1,0:T(8,128)(2,1)} %constant_dynamic-update-slice_fusion, f32[128]{0:T(128)} %divide_subtract_fusion, f32[3456]{0:T(1024)S(1)} %convert_element_type.40), kind=kOutput, calls=%fused_computation.7 | convolution fusion | flops 910016512 | bytes 10631168 | tf_op jit(solution)/shard_map/dot_general | solution.py:72
  112.5 2.1 slice.21
  114.6 2.9 %reshape.165 = bf16[3328,128]{1,0:T(8,128)(2,1)} reshape(bf16[128,3328]{1,0:T(8,128)(2,1)} %slice.21) | data formatting | bytes 1703936 | tf_op jit(solution)/shard_map/reshape | solution.py:77
  117.5 14.9 %scatter_custom_fusion.1 = bf16[4992,128]{1,0:T(8,128)(2,1)} fusion(s32[3328]{0:T(1024)} %copy-done.2, bf16[3328,128]{1,0:T(8,128)(2,1)} %reshape.165, bf16[]{:T(256)} %constant.5.clone.1), kind=kCustom, calls=%fused_computation.21 | custom fusion | bytes 1278464 | tf_op jit(solution)/shard_map/scatter | solution.py:79
  132.3 4.3 %all-to-all-start.2 = ((bf16[8,624,128]{2,1,0:T(8,128)(2,1)}), bf16[8,624,128]{2,1,0:T(8,128)(2,1)}, u32[]{:S(2)}, u32[]{:S(2)}) async-start(bf16[8,624,128]{2,1,0:T(8,128)(2,1)} %bitcast.33), calls=%async_computation.2 | async-start | bytes 2555904 | tf_op jit(solution)/shard_map/all_to_all | solution.py:81
  141.0 13.4 %all-to-all-done.2 = bf16[8,624,128]{2,1,0:T(8,128)(2,1)} async-done(((bf16[8,624,128]{2,1,0:T(8,128)(2,1)}), bf16[8,624,128]{2,1,0:T(8,128)(2,1)}, u32[]{:S(2)}, u32[]{:S(2)}) %all-to-all-start.2) | async-done | bytes 1277984 | tf_op jit(solution)/shard_map/all_to_all | solution.py:81
  154.5 33.9 %scatter_custom_fusion.2 = f32[2496,128]{1,0:T(8,128)} fusion(s32[4992]{0:T(1024)} %fusion.21, bf16[4992,128]{1,0:T(8,128)(2,1)} %bitcast.8, f32[]{:T(128)} %constant.9.clone.1), kind=kCustom, calls=%fused_computation.9 | custom fusion | flops 1277952 | bytes 2556416 | tf_op jit(solution)/shard_map/scatter-add | solution.py:91
  188.4 2.2 convert_element_type.47
  192.0 1.5 fusion.3
  193.5 43.2 %all-gather.1 = f32[32,1,3456]{2,1,0:T(1,128)} all-gather(f32[1,1,3456]{2,1,0:T(1,128)S(1)} %reshape.179), channel_id=2, replica_groups=mesh['grp'=4,'emb'=8] {'grp','emb'}, dimensions={0}, use_global_device_ids=true | all-gather | bytes 456192 | tf_op jit(solution)/shard_map/all_gather | solution.py:8
  236.7 1.9 reduce_sum.52
  238.6 2.3 reshape.135
  (32 shorter events, 23.6 us)
Async XLA Ops:
  7.2 92.5 %copy-start = (bf16[3456,512]{1,0:T(8,128)(2,1)S(1)}, bf16[3456,512]{1,0:T(8,128)(2,1)}, u32[]{:S(2)}) copy-start(bf16[3456,512]{1,0:T(8,128)(2,1)} %param.17) | copy-start | bytes 10616836
  22.2 41.2 %copy-start.2 = (s32[3328]{0:T(1024)}, s32[3328]{0:T(1024)S(1)}, u32[]{:S(2)}) copy-start(s32[3328]{0:T(1024)S(1)} %fusion.22) | copy-start | bytes 39940
  47.1 0.6 copy-start.1
  63.4 22.1 %all-to-all-start.1 = ((bf16[8,624,128]{2,1,0:T(8,128)(2,1)}), bf16[8,624,128]{2,1,0:T(8,128)(2,1)}, u32[]{:S(2)}, u32[]{:S(2)}) async-start(bf16[8,624,128]{2,1,0:T(8,128)(2,1)} %bitcast.34), calls=%async_computation.1 | async-start | bytes 2555904 | tf_op jit(solution)/shard_map/all_to_all | solution.py:47
  132.3 22.1 %all-to-all-start.2 = ((bf16[8,624,128]{2,1,0:T(8,128)(2,1)}), bf16[8,624,128]{2,1,0:T(8,128)(2,1)}, u32[]{:S(2)}, u32[]{:S(2)}) async-start(bf16[8,624,128]{2,1,0:T(8,128)(2,1)} %bitcast.33), calls=%async_computation.2 | async-start | bytes 2555904 | tf_op jit(solution)/shard_map/all_to_all | solution.py:81
  136.6 102.0 %all-reduce.2.cloned.1.call-start = ((), (), s32[]{:S(2)}) async-start(), calls=%async_computation.3 | async-start | bytes 1277952 | tf_op jit(solution)/shard_map/psum | solution.py:93
Sparse Core Ops, SparseCore 0:
  190.7 40.6 all-reduce.1
